TPU v7x, 256 devices: a whole 4x4x8 slice. The times are simulated.
256 devices in a mesh: rows: 64 (over x, z, core), rep: 4 (over y).
Axes of the slice: x: 4, y: 4, z: 8, core: 2. Of those that a mesh axis runs over, the one named last changes fastest.
Arguments:
- a_vals: float32 [4, 512, 4, 128, 128], P('rep', 'rows'), may hold values from -0.25 to 0.25
- a_tgt: int32 [4, 512, 4], P('rep', 'rows'), may hold values from 0 to 9, all different within a row
- b_vals: float32 [512, 128, 12, 128], P(('rows', 'rep')), may hold values from -6 to 6
- b_cols: int32 [64, 12], P('rows'), may hold values from 0 to 511, as said below
- c_cols: int32 [512, 8], P(('rows', 'rep')), may hold values from 0 to 511, as said below
- c_count: int32 [512], P(('rows', 'rep')), may hold values from 1 to 8, 2560 in all
Outputs:
- c_vals: float32 [512, 8, 128, 128], P(('rows', 'rep'))
- row_start: int32 [512], P(('rows', 'rep'))
Inputs may be any that keep to these rules, and one draw needn't show every extreme that they name: `b_cols`: row g holds 12 distinct columns, each (g * 8 + 8 // 2 - 8 + o) mod 512 with o in 0 to 15. `c_cols`: row i holds 8 distinct columns, each ((i // 8) * 8 + 8 // 2 - 2 * 8 - 8 + o) mod 512 with o in 0 to 47. `a_tgt`: the 4 targets of one quarter and block column are distinct. `c_count`: the counts sum to 2560.
All inputs are finite; a program needn't handle non-finite values. No bound on the sum of `c_count` on one device may be relied on, other than what follows from the above.
Results may differ from a plain program's by a relative error of at most 0.0003.
Values sent between devices are 32-bit elements; how exact they have to be, the bound alone decides.
No kernel may reach another device: no remote copies, remote signals or barrier semaphores. Data moves between devices by JAX's collectives and lax.ppermute only.
A program may use at most 128 MiB of HBM per device.

v0:
```python
import jax
import jax.numpy as jnp
from jax import lax
from jax.sharding import PartitionSpec as P

REACH = 2


highest = lax.Precision.HIGHEST


def shifted(value, axis, by):
    size = lax.axis_size(axis)
    return lax.ppermute(value, axis, [(i, (i + by) % size) for i in range(size)])


def carried_in(part, axis, combine, identity):
    place = lax.axis_index(axis)
    gathered = lax.all_gather(part, axis)
    state = jnp.zeros_like(part) + jnp.asarray(identity, part.dtype)

    def one(lap, state):
        return combine(state, lax.dynamic_index_in_dim(gathered, lap, 0, False))

    return lax.fori_loop(0, place, one, state)


def target_matrix(targets, target_count):
    return (targets[:, :, None] == jnp.arange(target_count, dtype=jnp.int32)[None, None, :]).astype(
        jnp.float32
    )


def add_counts(former, latter):
    return former + latter


def local(a_vals, a_tgt, b_vals, b_cols, c_cols, c_count):
    blocks = a_vals[0]
    targets = a_tgt[0]
    rows_dev = b_vals.shape[0]
    block_edge = b_vals.shape[1]
    b_slots = b_vals.shape[2]
    a_slots = blocks.shape[1]
    spread = 2 * REACH + 1
    target_count = spread * rows_dev
    b_piece = lax.all_gather(b_vals, "rep", axis=0, tiled=True)
    k_count = b_piece.shape[0]
    a_part = blocks.reshape(k_count, a_slots * block_edge, block_edge)
    chosen = target_matrix(targets, target_count)
    b_part = b_piece.reshape(k_count, block_edge, b_slots * block_edge)
    products = lax.dot_general(
        a_part,
        b_part,
        (((2,), (1,)), ((0,), (0,))),
        precision=highest,
        preferred_element_type=jnp.float32,
    )
    products = products.reshape(k_count, a_slots, block_edge, b_slots * block_edge)
    partial_value = jnp.einsum("kse,ksaj->eaj", chosen, products, precision=highest)
    partial_value = partial_value.reshape(spread, rows_dev, block_edge, b_slots, block_edge)
    own_cols = b_cols[0]
    slot_ids = jnp.arange(c_cols.shape[1], dtype=jnp.int32)
    pattern = jnp.where(slot_ids[None, :] < c_count[:, None], c_cols, -1)
    col_tags = own_cols.astype(jnp.float32)
    arrived = []
    sender_cols = []
    for hop_index in range(spread):
        shift_by = hop_index - REACH
        if shift_by == 0:
            arrived.append(partial_value[hop_index])
            sender_cols.append(own_cols)
        else:
            moved, moved_tags = shifted((partial_value[hop_index], col_tags), "rows", shift_by)
            arrived.append(moved)
            sender_cols.append(moved_tags.astype(jnp.int32))
    arrived = jnp.stack(arrived)
    sender_cols = jnp.stack(sender_cols)
    weights = (pattern[:, :, None, None] == sender_cols[None, None, :, :]).astype(jnp.float32)
    result = jnp.einsum("ucdt,duatb->ucab", weights, arrived, precision=highest)
    before = jnp.cumsum(c_count, dtype=jnp.int32) - c_count
    local_total = jnp.sum(c_count)
    earlier = carried_in(local_total, ("rows", "rep"), add_counts, jnp.zeros((), jnp.int32))
    row_start = earlier + before
    return (result, row_start)


def solution(mesh):
    in_specs = (
        P("rep", "rows", None, None, None),
        P("rep", "rows", None),
        P(("rows", "rep"), None, None, None),
        P("rows", None),
        P(("rows", "rep"), None),
        P(("rows", "rep")),
    )
    out_specs = (P(("rows", "rep"), None, None, None), P(("rows", "rep")))
    return jax.shard_map(local, mesh=mesh, in_specs=in_specs, out_specs=out_specs, check_vma=False)
```

profile of v0, /device:TPU:1, one launch (start us, length us, event | category | flops | bytes accessed | tf_op | source)
XLA Modules:
  0.0 673.2 jit_solution(17965845921452244917)
XLA Ops:
  7.2 0.0 copy-start
  7.2 0.0 all-gather.2.cloned.1.call-start
  7.2 0.7 all-gather.2.cloned.1.call-update
  7.9 73.8 %all-gather.2.cloned.1.call-done = f32[8,128,12,128]{3,1,2,0:T(8,128)} async-done(((f32[2,128,12,128]{3,1,2,0:T(8,128)}), f32[8,128,12,128]{3,1,2,0:T(8,128)}) %all-gather.2.cloned.1.call-update) | async-done | bytes 6291472 | tf_op jit(solution)/shard_map/all_gather | solution.py:47
  81.7 6.6 copy.30
  88.2 0.0 copy-done
  88.2 0.0 copy-start.2
  88.2 21.9 %fusion.14 = f32[8,512,1536]{2,1,0:T(8,128)S(1)} fusion(f32[8,512,128]{2,1,0:T(8,128)S(1)} %bitcast.53, f32[8,128,1536]{1,2,0:T(8,128)} %bitcast.55), kind=kOutput, calls=%fused_computation.25 | convolution fusion | flops 9663676416 | bytes 33554432 | tf_op jit(solution)/shard_map/dot_general | solution.py:52
  110.1 0.0 copy-done.2
  110.2 21.9 %fusion.2 = f32[10,128,1536]{2,0,1:T(8,128)} fusion(f32[8,4,128,1536]{3,2,1,0:T(8,128)S(1)} %bitcast.54, s32[8,4]{0,1:T(4,128)S(1)} %bitcast.61), kind=kOutput, calls=%fused_computation.2 | convolution fusion | flops 754975040 | bytes 33030272 | tf_op jit(solution)/shard_map/kse,ksaj->eaj/dot_general | solution.py:60
  132.1 14.7 %fusion.13 = (f32[2,128,1536]{2,0,1:T(2,128)}, f32[2,128,1536]{2,0,1:T(2,128)}, f32[2,128,1536]{2,0,1:T(2,128)}, f32[2,128,1536]{2,0,1:T(2,128)}, f32[2,128,1536]{2,0,1:T(2,128)}) fusion(f32[10,128,1536]{2,0,1:T(8,128)} %fusion.2), kind=kLoop, calls=%fused_computation.24 | loop fusion | bytes 15728640 | tf_op jit(solution)/shard_map/slice | solution.py:74
  146.7 2.5 copy.33
  149.3 0.0 copy-start.5
  149.3 0.0 copy-start.3
  149.3 1.6 copy.34
  150.9 5.2 collective-permute-start.4
  156.1 0.0 copy-done.5
  156.1 0.0 collective-permute-start.3
  156.1 0.1 collective-permute-start.2
  156.2 1.4 collective-permute-start.1
  157.5 0.0 copy-done.3
  157.5 0.7 reduce_sum.9
  158.2 0.2 reduce-window.9
  158.4 0.7 dynamic-update-slice
  159.2 99.5 %all-reduce = s32[256]{0:T(256)S(1)} all-reduce(s32[256]{0:T(256)S(1)} %dynamic-update-slice), channel_id=1, replica_groups=mesh['rows'=64,'rep'=4] {'rows','rep'}, use_global_device_ids=true, to_apply=%add | all-reduce | flops 256 | bytes 2048
  258.6 5.2 while.10
  258.6 0.6 dynamic_slice.5
  259.9 0.7 dynamic_slice.5
  261.2 0.7 dynamic_slice.5
  262.6 0.7 dynamic_slice.5
  263.9 2.5 copy.36
  266.4 0.0 copy-start.4
  266.4 1.6 copy.37
  268.0 0.0 collective-permute-start.5
  268.0 0.5 fusion.12
  268.5 0.0 copy-done.4
  268.5 0.1 compare_select_fusion
  268.6 2.5 copy.40
  271.1 1.6 copy.41
  272.8 0.0 collective-permute-done.3
  272.8 7.6 %collective-permute-start.6 = (f32[2,128,12,128]{3,1,2,0:T(8,128)}, f32[2,128,12,128]{3,1,2,0:T(8,128)}, u32[]{:S(2)}, u32[]{:S(2)}) collective-permute-start(f32[2,128,12,128]{3,1,2,0:T(8,128)} %copy.41), channel_id=1, source_target_pairs={{0,4},{4,8},{8,12},{12,16},{16,20},{20,24},{24,28},{28,32},{32,36}... | collective-permute-start | bytes 4718600 | tf_op jit(solution)/shard_map/ppermute | solution.py:14
  280.3 0.0 collective-permute-done.2
  280.3 325.5 %collective-permute-start = (f32[12]{0:T(128)S(1)}, f32[12]{0:T(128)S(1)}, u32[]{:S(2)}, u32[]{:S(2)}) collective-permute-start(f32[12]{0:T(128)S(1)} %convert_bitcast_fusion.4), channel_id=1, source_target_pairs={{0,248},{4,252},{8,0},{12,4},{16,8},{20,12},{24,16},{28,20},{32,24... | collective-permute-start | bytes 152 | tf_op jit(solution)/shard_map/ppermute | solution.py:14
  605.9 2.5 copy.43
  608.4 1.6 copy.44
  610.0 0.0 collective-permute-done.1
  610.0 0.2 collective-permute-start.7
  610.2 0.0 collective-permute-done
  610.3 3.7 copy.39
  614.0 2.1 copy.46
  616.1 0.0 collective-permute-done.4
  616.1 2.3 bitcast_dynamic-update-slice_fusion.3
  618.5 0.0 collective-permute-done.5
  618.5 2.3 bitcast_dynamic-update-slice_fusion.2
  620.8 0.1 constant_dynamic-update-slice_fusion
  620.9 0.0 collective-permute-done.6
  621.0 2.3 bitcast_dynamic-update-slice_fusion.1
  623.3 34.4 %collective-permute-done.7 = f32[2,128,12,128]{3,1,2,0:T(8,128)} collective-permute-done((f32[2,128,12,128]{3,1,2,0:T(8,128)}, f32[2,128,12,128]{3,1,2,0:T(8,128)}, u32[]{:S(2)}, u32[]{:S(2)}) %collective-permute-start.7) | collective-permute-done | bytes 1572896 | tf_op jit(solution)/shard_map/ppermute | solution.py:14
  657.7 2.3 bitcast_dynamic-update-slice_fusion
  660.0 0.0 copy-start.1
  660.0 5.0 convolution_bitcast_fusion
  665.0 1.2 copy.47
  666.1 0.0 copy-done.1
  (7 shorter events, 0.0 us)
Async XLA Ops:
  7.2 81.1 %copy-start = (f32[1,8,4,128,128]{4,3,2,1,0:T(8,128)S(1)}, f32[1,8,4,128,128]{4,3,2,1,0:T(8,128)}, u32[]{:S(2)}) copy-start(f32[1,8,4,128,128]{4,3,2,1,0:T(8,128)} %param.8) | copy-start | bytes 6291460
  7.2 74.5 %all-gather.2.cloned.1.call-start = ((), (), s32[]{:S(2)}) async-start(), calls=%async_computation | async-start | bytes 7864320 | tf_op jit(solution)/shard_map/all_gather | solution.py:47
  88.2 21.9 %copy-start.2 = (s32[1,8,4]{1,2,0:T(4,128)S(1)}, s32[1,8,4]{1,2,0:T(4,128)}, u32[]{:S(2)}) copy-start(s32[1,8,4]{1,2,0:T(4,128)} %param.9) | copy-start | bytes 388
  149.3 6.8 %copy-start.5 = (s32[1,12]{1,0:T(1,128)S(1)}, s32[1,12]{1,0:T(1,128)}, u32[]{:S(2)}) copy-start(s32[1,12]{1,0:T(1,128)} %param.11) | copy-start | bytes 148
  149.3 8.3 %copy-start.3 = (s32[2]{0:T(128)S(1)}, s32[2]{0:T(128)}, u32[]{:S(2)}) copy-start(s32[2]{0:T(128)} %param.13) | copy-start | bytes 28
  150.9 465.2 %collective-permute-start.4 = (f32[2,128,12,128]{3,1,2,0:T(8,128)}, f32[2,128,12,128]{3,1,2,0:T(8,128)}, u32[]{:S(2)}, u32[]{:S(2)}) collective-permute-start(f32[2,128,12,128]{3,1,2,0:T(8,128)} %copy.34), channel_id=1, source_target_pairs={{0,248},{4,252},{8,0},{12,4},{16,8},{20,12},{24,16},{28,20},{32,24... | collective-permute-start | bytes 4718600 | tf_op jit(solution)/shard_map/ppermute | solution.py:14
  156.1 116.7 %collective-permute-start.3 = (f32[12]{0:T(128)S(1)}, f32[12]{0:T(128)S(1)}, u32[]{:S(2)}, u32[]{:S(2)}) collective-permute-start(f32[12]{0:T(128)S(1)} %convert_bitcast_fusion.4), channel_id=1, source_target_pairs={{0,8},{4,12},{8,16},{12,20},{16,24},{20,28},{24,32},{28,36},{32,40... | collective-permute-start | bytes 152 | tf_op jit(solution)/shard_map/ppermute | solution.py:14
  156.1 124.3 %collective-permute-start.2 = (f32[12]{0:T(128)S(1)}, f32[12]{0:T(128)S(1)}, u32[]{:S(2)}, u32[]{:S(2)}) collective-permute-start(f32[12]{0:T(128)S(1)} %convert_bitcast_fusion.4), channel_id=1, source_target_pairs={{0,4},{4,8},{8,12},{12,16},{16,20},{20,24},{24,28},{28,32},{32,36}... | collective-permute-start | bytes 152 | tf_op jit(solution)/shard_map/ppermute | solution.py:14
  156.2 453.8 %collective-permute-start.1 = (f32[12]{0:T(128)S(1)}, f32[12]{0:T(128)S(1)}, u32[]{:S(2)}, u32[]{:S(2)}) collective-permute-start(f32[12]{0:T(128)S(1)} %convert_bitcast_fusion.4), channel_id=1, source_target_pairs={{0,252},{4,0},{8,4},{12,8},{16,12},{20,16},{24,20},{28,24},{32,28}... | collective-permute-start | bytes 152 | tf_op jit(solution)/shard_map/ppermute | solution.py:14
  266.4 2.2 copy-start.4
  268.0 350.4 %collective-permute-start.5 = (f32[2,128,12,128]{3,1,2,0:T(8,128)}, f32[2,128,12,128]{3,1,2,0:T(8,128)}, u32[]{:S(2)}, u32[]{:S(2)}) collective-permute-start(f32[2,128,12,128]{3,1,2,0:T(8,128)} %copy.37), channel_id=1, source_target_pairs={{0,252},{4,0},{8,4},{12,8},{16,12},{20,16},{24,20},{28,24},{32,28}... | collective-permute-start | bytes 4718600 | tf_op jit(solution)/shard_map/ppermute | solution.py:14
  272.8 348.2 %collective-permute-start.6 = (f32[2,128,12,128]{3,1,2,0:T(8,128)}, f32[2,128,12,128]{3,1,2,0:T(8,128)}, u32[]{:S(2)}, u32[]{:S(2)}) collective-permute-start(f32[2,128,12,128]{3,1,2,0:T(8,128)} %copy.41), channel_id=1, source_target_pairs={{0,4},{4,8},{8,12},{12,16},{16,20},{20,24},{24,28},{28,32},{32,36}... | collective-permute-start | bytes 4718600 | tf_op jit(solution)/shard_map/ppermute | solution.py:14
  280.3 329.9 %collective-permute-start = (f32[12]{0:T(128)S(1)}, f32[12]{0:T(128)S(1)}, u32[]{:S(2)}, u32[]{:S(2)}) collective-permute-start(f32[12]{0:T(128)S(1)} %convert_bitcast_fusion.4), channel_id=1, source_target_pairs={{0,248},{4,252},{8,0},{12,4},{16,8},{20,12},{24,16},{28,20},{32,24... | collective-permute-start | bytes 152 | tf_op jit(solution)/shard_map/ppermute | solution.py:14
  610.0 47.7 %collective-permute-start.7 = (f32[2,128,12,128]{3,1,2,0:T(8,128)}, f32[2,128,12,128]{3,1,2,0:T(8,128)}, u32[]{:S(2)}, u32[]{:S(2)}) collective-permute-start(f32[2,128,12,128]{3,1,2,0:T(8,128)} %copy.44), channel_id=1, source_target_pairs={{0,8},{4,12},{8,16},{12,20},{16,24},{20,28},{24,32},{28,36},{32,40... | collective-permute-start | bytes 4718600 | tf_op jit(solution)/shard_map/ppermute | solution.py:14
  660.0 6.1 copy-start.1
Sparse Core Ops, SparseCore 0:
  9.8 71.8 all-gather.1
where the time goes:
time: 685 us; the launch traced here: 673 us
  starting transfers between devices  340 us (50%)
  waiting for transfers between devices  109 us (16%)
  blocking collectives  99.5 us (15%)
  local copies, waits for them, and re-layouts  57.6 us (8%)
  matrix products  48.8 us (7%)
  between operations  14.5 us (2%)
    ppermute x8, starting transfers between devices, shifted(): lax.ppermute(value, axis, [(i, (i + by) % size) for i in range(size)])  340 us
    unnamed x1, blocking collectives  99.5 us
    all_gather x1, waiting for transfers between devices, local(): b_piece = lax.all_gather(b_vals, 'rep', axis=0, tiled=True)  73.8 us
    ppermute x8, waiting for transfers between devices, shifted(): lax.ppermute(value, axis, [(i, (i + by) % size) for i in range(size)])  34.4 us
    slice x5, local copies, waits for them, and re-layouts, local(): partial_value[hop_index]  24.7 us
    dot_general x1, matrix products, local(): lax.dot_general(a_part, b_part, (((2,), (1,)), ((0,), (0,))), precision=h...  21.9 us
    dot_general x1, matrix products, local(): jnp.einsum('kse,ksaj->eaj', chosen, products, precision=highest)  21.9 us
  transfers between devices with their start and end apart: 9, of which 2 were waited for; matrix products, arithmetic and copies ran while one was open for 4% of the time, Pallas kernels for 0%

commit v1 on v0

v1 whole, which is shorter than its diff:
```python
import jax
import jax.numpy as jnp
from jax import lax
from jax.sharding import PartitionSpec as P

REACH = 2
COUNT_PAD = 1024

highest = lax.Precision.HIGHEST
high = lax.Precision.HIGH


def shifted(value, axis, by):
    size = lax.axis_size(axis)
    return lax.ppermute(value, axis, [(i, (i + by) % size) for i in range(size)])


def earlier_counts(c_count):
    padded = jnp.zeros((COUNT_PAD,), jnp.int32).at[: c_count.shape[0]].set(c_count)
    gathered = lax.all_gather(padded, ("rows", "rep"), axis=0)
    all_counts = gathered[:, : c_count.shape[0]].reshape(-1)
    first_row = lax.axis_index(("rows", "rep")) * c_count.shape[0]
    row_ids = jnp.arange(all_counts.shape[0], dtype=jnp.int32)
    return jnp.sum(jnp.where(row_ids < first_row, all_counts, 0))


def local(a_vals, a_tgt, b_vals, b_cols, c_cols, c_count):
    blocks = a_vals[0]
    targets = a_tgt[0]
    rows_dev = b_vals.shape[0]
    block_edge = b_vals.shape[1]
    b_slots = b_vals.shape[2]
    k_count = blocks.shape[0]
    spread = 2 * REACH + 1
    target_count = spread * rows_dev
    n_rep = lax.axis_size("rep")
    place = lax.axis_index("rep")

    hit = targets[None, :, :] == jnp.arange(target_count, dtype=jnp.int32)[:, None, None]
    selected = jnp.sum(jnp.where(hit[:, :, :, None, None], blocks[None], 0.0), axis=2)

    def chunk_product(b_chunk, source):
        a_chunk = lax.dynamic_slice_in_dim(selected, source * rows_dev, rows_dev, 1)
        b_flat = b_chunk.reshape(rows_dev, block_edge, b_slots * block_edge)
        return lax.dot_general(
            a_chunk,
            b_flat,
            (((1, 3), (0, 1)), ((), ())),
            precision=high,
            preferred_element_type=jnp.float32,
        )

    partial_value = chunk_product(b_vals, place)
    for by in range(1, n_rep):
        arrived_b = shifted(b_vals, "rep", by)
        partial_value = partial_value + chunk_product(arrived_b, (place - by) % n_rep)
    partial_value = partial_value.reshape(spread, rows_dev, block_edge, b_slots, block_edge)

    own_cols = b_cols[0]
    slot_ids = jnp.arange(c_cols.shape[1], dtype=jnp.int32)
    pattern = jnp.where(slot_ids[None, :] < c_count[:, None], c_cols, -1)
    col_tags = own_cols.astype(jnp.float32)
    arrived = []
    sender_cols = []
    for hop_index in range(spread):
        shift_by = hop_index - REACH
        if shift_by == 0:
            arrived.append(partial_value[hop_index])
            sender_cols.append(own_cols)
        else:
            moved, moved_tags = shifted((partial_value[hop_index], col_tags), "rows", shift_by)
            arrived.append(moved)
            sender_cols.append(moved_tags.astype(jnp.int32))
    arrived = jnp.stack(arrived)
    sender_cols = jnp.stack(sender_cols)
    weights = (pattern[:, :, None, None] == sender_cols[None, None, :, :]).astype(jnp.float32)
    result = jnp.einsum("ucdt,duatb->ucab", weights, arrived, precision=highest)
    before = jnp.cumsum(c_count, dtype=jnp.int32) - c_count
    row_start = earlier_counts(c_count) + before
    return (result, row_start)


def solution(mesh):
    in_specs = (
        P("rep", "rows", None, None, None),
        P("rep", "rows", None),
        P(("rows", "rep"), None, None, None),
        P("rows", None),
        P(("rows", "rep"), None),
        P(("rows", "rep")),
    )
    out_specs = (P(("rows", "rep"), None, None, None), P(("rows", "rep")))
    return jax.shard_map(local, mesh=mesh, in_specs=in_specs, out_specs=out_specs, check_vma=False)
```

time: 685 us -> 215 us (0.31); the launches traced: 673 us -> 212 us
  starting transfers between devices: 340 us -> 23.3 us
  blocking collectives: 99.5 us -> 0 us
  local copies, waits for them, and re-layouts: 57.6 us -> 38.6 us
  matrix products: 48.8 us -> 31.1 us
  waiting for transfers between devices: 109 us -> 95.3 us
  other arithmetic: 1.47 us -> 8.98 us
    ppermute x8 -> x11, starting transfers between devices: 340 us -> 23.3 us  [shifted(): lax.ppermute(value, axis, [(i, (i + by) % size) for i in range(size)])]
    unnamed x1 -> x0, blocking collectives: 99.5 us -> none
    all_gather x1, waiting for transfers between devices: 73.8 us -> 0.02 us  [earlier_counts(): gathered = lax.all_gather(padded, ('rows', 'rep'), axis=0)]
    ppermute x8 -> x11, waiting for transfers between devices: 34.4 us -> 95.2 us  [shifted(): lax.ppermute(value, axis, [(i, (i + by) % size) for i in range(size)])]
    dot_general x2 -> x4, matrix products: 43.8 us -> 26.1 us  [chunk_product(): lax.dot_general(a_chunk, b_flat, (((1, 3), (0, 1)), ((), ())), precision=...]
    slice x5, local copies, waits for them, and re-layouts: 24.7 us -> 13.7 us  [local(): partial_value[hop_index]]
    reduce_sum x1 -> x2, other arithmetic: 0.7 us -> 7.55 us  [the longest x1 6.88 us: local(): jnp.sum(jnp.where(hit[:, :, :, None, None], blocks[None], 0.0), axis=2)]
  transfers between devices with their start and end apart: 9 -> 12, of which waited for: 2 -> 5; matrix products, arithmetic and copies ran while one was open for 4% -> 32% of each run, Pallas kernels for 0% -> 0%
where the time goes in v1:
time: 215 us; the launch traced here: 212 us
  waiting for transfers between devices  95.3 us (44%)
  local copies, waits for them, and re-layouts  38.6 us (18%)
  matrix products  31.1 us (14%)
  starting transfers between devices  23.3 us (11%)
  between operations  14.4 us (7%)
  other arithmetic  8.98 us (4%)
    ppermute x11, waiting for transfers between devices, shifted(): lax.ppermute(value, axis, [(i, (i + by) % size) for i in range(size)])  95.2 us
    dot_general x4, matrix products, chunk_product(): lax.dot_general(a_chunk, b_flat, (((1, 3), (0, 1)), ((), ())), precision=...  26.1 us
    ppermute x11, starting transfers between devices, shifted(): lax.ppermute(value, axis, [(i, (i + by) % size) for i in range(size)])  23.3 us
    slice x5, local copies, waits for them, and re-layouts, local(): partial_value[hop_index]  13.7 us
    unnamed x18, local copies, waits for them, and re-layouts  12.2 us
    reduce_sum x1, other arithmetic, local(): jnp.sum(jnp.where(hit[:, :, :, None, None], blocks[None], 0.0), axis=2)  6.88 us
    squeeze x4, local copies, waits for them, and re-layouts, local(): partial_value[hop_index]  6.51 us
    dot_general x1, matrix products, local(): result = jnp.einsum('ucdt,duatb->ucab', weights, arrived, precision=highest)  4.95 us
  transfers between devices with their start and end apart: 12, of which 5 were waited for; matrix products, arithmetic and copies ran while one was open for 32% of the time, Pallas kernels for 0%

profile of v1, /device:TPU:1, one launch (start us, length us, event | category | flops | bytes accessed | tf_op | source)
XLA Modules:
  0.0 211.7 jit_solution(7734660871240010261)
XLA Ops:
  7.2 0.0 copy-start.1
  7.2 0.0 copy-start.2
  7.2 0.0 all-gather.3.cloned.1.call-start
  7.2 1.9 copy.59
  9.1 3.8 %collective-permute-start.5 = (f32[2,128,12,128]{1,3,2,0:T(8,128)S(1)}, f32[2,128,12,128]{1,3,2,0:T(8,128)}, u32[]{:S(2)}, u32[]{:S(2)}) collective-permute-start(f32[2,128,12,128]{1,3,2,0:T(8,128)S(1)} %copy.59), channel_id=1, source_target_pairs={{0,2},{1,3},{2,0},{3,1},{4,6},{5,7},{6,4},{7,5},{8,10},{9,11},{10,... | collective-permute-start | bytes 4718600 | tf_op jit(solution)/shard_map/ppermute | solution.py:15
  12.9 0.8 collective-permute-start.6
  13.7 1.1 collective-permute-start.4
  14.8 0.0 copy-done.1
  14.8 0.6 pad_bitcast_fusion
  15.4 0.0 all-gather.3.cloned.1.call-update
  15.5 0.0 copy-done.2
  15.5 0.1 copy.58
  15.6 6.9 %select_reduce_fusion = f32[10,8,128,128]{3,2,1,0:T(8,128)} fusion(f32[8,4,128,128]{3,2,1,0:T(8,128)} %bitcast.83, pred[10,8,4]{2,1,0:T(8,128)(4,1)S(1)} %iota_compare_fusion), kind=kLoop, calls=%fused_computation | loop fusion | flops 9175040 | bytes 7340352 | tf_op jit(solution)/shard_map/reduce_sum | solution.py:40
  22.4 4.9 %fusion.5 = f32[10,128,1536,1]{2,1,3,0:T(8,128)S(1)} fusion(f32[2,128,1536,1]{1,2,0,3:T(8,128)S(1)} %bitcast.77, f32[10,8,128,128]{3,2,1,0:T(8,128)} %select_reduce_fusion, s32[]{:T(128)S(6)} %select_n.42), kind=kOutput, calls=%fused_computation.14 | convolution fusion | flops 3019898880 | bytes 10747908 | tf_op jit(solution)/shard_map/dot_general | solution.py:45
  27.3 18.7 %collective-permute-done.5 = f32[2,128,12,128]{1,3,2,0:T(8,128)} collective-permute-done((f32[2,128,12,128]{1,3,2,0:T(8,128)S(1)}, f32[2,128,12,128]{1,3,2,0:T(8,128)}, u32[]{:S(2)}, u32[]{:S(2)}) %collective-permute-start.5) | collective-permute-done | bytes 1572896 | tf_op jit(solution)/shard_map/ppermute | solution.py:15
  46.1 0.0 copy-done
  46.1 5.1 %fusion.1 = f32[10,128,1536,1]{2,1,3,0:T(8,128)S(1)} fusion(f32[2,128,1536,1]{1,2,0,3:T(8,128)} %bitcast.18, f32[10,8,128,128]{3,2,1,0:T(8,128)S(1)} %copy-done, s32[]{:T(128)S(6)} %select_n.46), kind=kOutput, calls=%fused_computation.10 | convolution fusion | flops 3019898880 | bytes 10747908 | tf_op jit(solution)/shard_map/dot_general | solution.py:45
  51.1 30.5 %collective-permute-done.4 = f32[2,128,12,128]{1,3,2,0:T(8,128)} collective-permute-done((f32[2,128,12,128]{1,3,2,0:T(8,128)S(1)}, f32[2,128,12,128]{1,3,2,0:T(8,128)}, u32[]{:S(2)}, u32[]{:S(2)}) %collective-permute-start.4) | collective-permute-done | bytes 1572896 | tf_op jit(solution)/shard_map/ppermute | solution.py:15
  81.6 7.0 %fusion.3 = f32[10,128,1536,1]{2,1,3,0:T(8,128)} fusion(f32[2,128,1536,1]{1,2,0,3:T(8,128)} %bitcast.14, f32[10,8,128,128]{3,2,1,0:T(8,128)S(1)} %copy-done, s32[]{:T(128)S(6)} %select_n.44), kind=kOutput, calls=%fused_computation.12 | convolution fusion | flops 3019898880 | bytes 10747908 | tf_op jit(solution)/shard_map/dot_general | solution.py:45
  88.6 0.0 collective-permute-done.6
  88.6 9.3 %bitcast_add_fusion = f32[10,128,1536]{2,1,0:T(8,128)} fusion(f32[10,128,1536,1]{2,1,3,0:T(8,128)S(1)} %fusion.1, f32[10,128,1536,1]{2,1,3,0:T(8,128)} %fusion.3, f32[10,128,1536,1]{2,1,3,0:T(8,128)S(1)} %fusion.5, f32[2,128,1536,1]{1,2,0,3:T(8,128)S(1)} %bitcast.84, f32[10,8,128,128]{3,2,1,0:T(8,128)} %select_reduce_fusion, s32[]{:T(128)S(6)} %select_n.48), kind=kOutput, calls=%fused_computation.1 | convolution fusion | flops 3025797120 | bytes 34340868 | tf_op jit(solution)/shard_map/dot_general | solution.py:45
  97.9 6.2 %fusion.17 = (f32[2,128,1536]{2,1,0:T(8,128)}, f32[2,128,1536]{2,1,0:T(8,128)}, f32[2,128,1536]{2,1,0:T(8,128)S(1)}, f32[2,128,1536]{2,1,0:T(8,128)}, f32[2,128,1536]{2,1,0:T(8,128)}) fusion(f32[10,128,1536]{2,1,0:T(8,128)} %bitcast_add_fusion), kind=kLoop, calls=%fused_computation.39 | loop fusion | bytes 15728640 | tf_op jit(solution)/shard_map/slice | solution.py:71
  104.1 1.9 copy.67
  106.0 0.0 copy-start.4
  106.0 0.0 copy-start.3
  106.0 1.6 copy.68
  107.6 7.9 %collective-permute-start.7 = (f32[2,128,12,128]{3,1,2,0:T(8,128)}, f32[2,128,12,128]{3,1,2,0:T(8,128)}, u32[]{:S(2)}, u32[]{:S(2)}) collective-permute-start(f32[2,128,12,128]{3,1,2,0:T(8,128)} %copy.68), channel_id=1, source_target_pairs={{0,248},{4,252},{8,0},{12,4},{16,8},{20,12},{24,16},{28,20},{32,24... | collective-permute-start | bytes 4718600 | tf_op jit(solution)/shard_map/ppermute | solution.py:15
  115.5 0.0 copy-done.4
  115.5 0.0 collective-permute-start.3
  115.5 0.1 collective-permute-start.2
  115.6 0.8 collective-permute-start.1
  116.5 0.1 compare_select_fusion
  116.5 1.9 copy.70
  118.4 1.6 copy.71
  120.0 5.0 %collective-permute-start.8 = (f32[2,128,12,128]{3,1,2,0:T(8,128)}, f32[2,128,12,128]{3,1,2,0:T(8,128)}, u32[]{:S(2)}, u32[]{:S(2)}) collective-permute-start(f32[2,128,12,128]{3,1,2,0:T(8,128)} %copy.71), channel_id=1, source_target_pairs={{0,252},{4,0},{8,4},{12,8},{16,12},{20,16},{24,20},{28,24},{32,28}... | collective-permute-start | bytes 4718600 | tf_op jit(solution)/shard_map/ppermute | solution.py:15
  125.0 0.2 reduce-window.9
  125.2 0.0 collective-permute-done.3
  125.2 1.7 collective-permute-start
  126.9 0.0 collective-permute-done.2
  126.9 1.9 copy.74
  128.7 1.6 copy.75
  130.4 0.5 collective-permute-start.9
  130.8 16.2 %collective-permute-done.1 = f32[12]{0:T(128)S(1)} collective-permute-done((f32[12]{0:T(128)S(1)}, f32[12]{0:T(128)S(1)}, u32[]{:S(2)}, u32[]{:S(2)}) %collective-permute-start.1) | collective-permute-done | bytes 80 | tf_op jit(solution)/shard_map/ppermute | solution.py:15
  147.0 1.9 copy.77
  148.9 1.6 copy.78
  150.5 1.6 collective-permute-start.10
  152.2 0.0 collective-permute-done
  152.2 1.6 copy.73
  153.8 2.1 %copy.80 = f32[1,2,128,12,128]{4,3,0,2,1:T(8,128)S(1)} copy(f32[1,2,128,12,128]{2,4,3,1,0:T(8,128)} %bitcast.82) | data formatting | bytes 3145728 | tf_op jit(solution)/shard_map/slice | solution.py:68
  156.0 0.0 all-gather.3.cloned.1.call-done
  156.0 1.4 copy.102
  157.4 0.7 fusion.7
  158.1 1.2 fusion.16
  159.3 0.0 collective-permute-done.7
  159.3 2.3 %bitcast_dynamic-update-slice_fusion.3 = f32[5,2,128,12,128]{4,3,0,2,1:T(8,128)S(1)} fusion(f32[2,128,12,128]{3,1,2,0:T(8,128)} %collective-permute-done.7), kind=kLoop, calls=%fused_computation.7 | loop fusion | bytes 3670016
  161.6 2.3 %collective-permute-done.8 = f32[2,128,12,128]{3,1,2,0:T(8,128)} collective-permute-done((f32[2,128,12,128]{3,1,2,0:T(8,128)}, f32[2,128,12,128]{3,1,2,0:T(8,128)}, u32[]{:S(2)}, u32[]{:S(2)}) %collective-permute-start.8) | collective-permute-done | bytes 1572896 | tf_op jit(solution)/shard_map/ppermute | solution.py:15
  163.9 2.3 %bitcast_dynamic-update-slice_fusion.2 = f32[5,2,128,12,128]{4,3,0,2,1:T(8,128)S(1)} fusion(f32[5,2,128,12,128]{4,3,0,2,1:T(8,128)S(1)} %bitcast_dynamic-update-slice_fusion.3, f32[2,128,12,128]{3,1,2,0:T(8,128)} %collective-permute-done.8), kind=kLoop, calls=%fused_computation.6 | loop fusion | bytes 3670016
  166.2 0.1 constant_dynamic-update-slice_fusion
  166.4 0.0 collective-permute-done.9
  166.4 2.3 %bitcast_dynamic-update-slice_fusion.1 = f32[5,2,128,12,128]{4,3,0,2,1:T(8,128)S(1)} fusion(f32[5,2,128,12,128]{4,3,0,2,1:T(8,128)S(1)} %constant_dynamic-update-slice_fusion, f32[2,128,12,128]{3,1,2,0:T(8,128)} %collective-permute-done.9), kind=kLoop, calls=%fused_computation.5 | loop fusion | bytes 3670016
  168.7 27.5 %collective-permute-done.10 = f32[2,128,12,128]{3,1,2,0:T(8,128)} collective-permute-done((f32[2,128,12,128]{3,1,2,0:T(8,128)}, f32[2,128,12,128]{3,1,2,0:T(8,128)}, u32[]{:S(2)}, u32[]{:S(2)}) %collective-permute-start.10) | collective-permute-done | bytes 1572896 | tf_op jit(solution)/shard_map/ppermute | solution.py:15
  196.2 2.3 %bitcast_dynamic-update-slice_fusion = f32[5,2,128,12,128]{4,3,0,2,1:T(8,128)S(1)} fusion(f32[5,2,128,12,128]{4,3,0,2,1:T(8,128)S(1)} %bitcast_dynamic-update-slice_fusion.1, f32[2,128,12,128]{3,1,2,0:T(8,128)} %collective-permute-done.10), kind=kLoop, calls=%fused_computation.4 | loop fusion | bytes 3670016 | tf_op jit(solution)/shard_map/stack | solution.py:74
  198.5 5.0 %convolution_bitcast_fusion = f32[2,8,128,128]{3,1,2,0:T(8,128)S(1)} fusion(f32[5,2,128,12,128]{4,3,0,2,1:T(8,128)S(1)} %bitcast_dynamic-update-slice_fusion, s32[5,12]{1,0:T(8,128)S(1)} %stack.34, s32[2,8]{1,0:T(2,128)S(1)} %compare_select_fusion), kind=kOutput, calls=%fused_computation.8 | convolution fusion | flops 188744640 | bytes 8913200 | tf_op jit(solution)/shard_map/ucdt,duatb->ucab/dot_general | solution.py:77
  203.5 1.2 copy.81
  (9 shorter events, 0.1 us)
Async XLA Ops:
  7.2 7.7 %copy-start.1 = (s32[2]{0:T(128)S(1)}, s32[2]{0:T(128)}, u32[]{:S(2)}) copy-start(s32[2]{0:T(128)} %param.13) | copy-start | bytes 28
  7.2 8.3 %copy-start.2 = (s32[1,8,4]{1,2,0:T(4,128)S(1)}, s32[1,8,4]{1,2,0:T(4,128)}, u32[]{:S(2)}) copy-start(s32[1,8,4]{1,2,0:T(4,128)} %param.9) | copy-start | bytes 388
  7.2 148.8 %all-gather.3.cloned.1.call-start = ((), (), s32[]{:S(2)}) async-start(), calls=%async_computation | async-start | bytes 1052672 | tf_op jit(solution)/shard_map/all_gather | solution.py:20
  9.1 37.0 %collective-permute-start.5 = (f32[2,128,12,128]{1,3,2,0:T(8,128)S(1)}, f32[2,128,12,128]{1,3,2,0:T(8,128)}, u32[]{:S(2)}, u32[]{:S(2)}) collective-permute-start(f32[2,128,12,128]{1,3,2,0:T(8,128)S(1)} %copy.59), channel_id=1, source_target_pairs={{0,2},{1,3},{2,0},{3,1},{4,6},{5,7},{6,4},{7,5},{8,10},{9,11},{10,... | collective-permute-start | bytes 4718600 | tf_op jit(solution)/shard_map/ppermute | solution.py:15
  12.9 75.7 %collective-permute-start.6 = (f32[2,128,12,128]{1,3,2,0:T(8,128)S(1)}, f32[2,128,12,128]{1,3,2,0:T(8,128)S(1)}, u32[]{:S(2)}, u32[]{:S(2)}) collective-permute-start(f32[2,128,12,128]{1,3,2,0:T(8,128)S(1)} %copy.59), channel_id=1, source_target_pairs={{0,3},{1,0},{2,1},{3,2},{4,7},{5,4},{6,5},{7,6},{8,11},{9,8},{10,9... | collective-permute-start | bytes 4718600 | tf_op jit(solution)/shard_map/ppermute | solution.py:15
  13.7 67.9 %collective-permute-start.4 = (f32[2,128,12,128]{1,3,2,0:T(8,128)S(1)}, f32[2,128,12,128]{1,3,2,0:T(8,128)}, u32[]{:S(2)}, u32[]{:S(2)}) collective-permute-start(f32[2,128,12,128]{1,3,2,0:T(8,128)S(1)} %copy.59), channel_id=1, source_target_pairs={{0,1},{1,2},{2,3},{3,0},{4,5},{5,6},{6,7},{7,4},{8,9},{9,10},{10,1... | collective-permute-start | bytes 4718600 | tf_op jit(solution)/shard_map/ppermute | solution.py:15
  22.4 23.6 %copy-start = (f32[10,8,128,128]{3,2,1,0:T(8,128)S(1)}, f32[10,8,128,128]{3,2,1,0:T(8,128)}, u32[]{:S(2)}) copy-start(f32[10,8,128,128]{3,2,1,0:T(8,128)} %select_reduce_fusion) | copy-start | bytes 15728644
  106.0 9.6 %copy-start.4 = (s32[1,12]{1,0:T(1,128)S(1)}, s32[1,12]{1,0:T(1,128)}, u32[]{:S(2)}) copy-start(s32[1,12]{1,0:T(1,128)} %param.11) | copy-start | bytes 148
  106.0 10.5 %copy-start.3 = (s32[2,8]{1,0:T(2,128)S(1)}, s32[2,8]{1,0:T(2,128)}, u32[]{:S(2)}) copy-start(s32[2,8]{1,0:T(2,128)} %param.12) | copy-start | bytes 196
  107.6 51.7 %collective-permute-start.7 = (f32[2,128,12,128]{3,1,2,0:T(8,128)}, f32[2,128,12,128]{3,1,2,0:T(8,128)}, u32[]{:S(2)}, u32[]{:S(2)}) collective-permute-start(f32[2,128,12,128]{3,1,2,0:T(8,128)} %copy.68), channel_id=1, source_target_pairs={{0,248},{4,252},{8,0},{12,4},{16,8},{20,12},{24,16},{28,20},{32,24... | collective-permute-start | bytes 4718600 | tf_op jit(solution)/shard_map/ppermute | solution.py:15
  115.5 9.7 %collective-permute-start.3 = (f32[12]{0:T(128)S(1)}, f32[12]{0:T(128)S(1)}, u32[]{:S(2)}, u32[]{:S(2)}) collective-permute-start(f32[12]{0:T(128)S(1)} %convert_bitcast_fusion.4), channel_id=1, source_target_pairs={{0,8},{4,12},{8,16},{12,20},{16,24},{20,28},{24,32},{28,36},{32,40... | collective-permute-start | bytes 152 | tf_op jit(solution)/shard_map/ppermute | solution.py:15
  115.5 11.3 %collective-permute-start.2 = (f32[12]{0:T(128)S(1)}, f32[12]{0:T(128)S(1)}, u32[]{:S(2)}, u32[]{:S(2)}) collective-permute-start(f32[12]{0:T(128)S(1)} %convert_bitcast_fusion.4), channel_id=1, source_target_pairs={{0,4},{4,8},{8,12},{12,16},{16,20},{20,24},{24,28},{28,32},{32,36}... | collective-permute-start | bytes 152 | tf_op jit(solution)/shard_map/ppermute | solution.py:15
  115.6 31.4 %collective-permute-start.1 = (f32[12]{0:T(128)S(1)}, f32[12]{0:T(128)S(1)}, u32[]{:S(2)}, u32[]{:S(2)}) collective-permute-start(f32[12]{0:T(128)S(1)} %convert_bitcast_fusion.4), channel_id=1, source_target_pairs={{0,252},{4,0},{8,4},{12,8},{16,12},{20,16},{24,20},{28,24},{32,28}... | collective-permute-start | bytes 152 | tf_op jit(solution)/shard_map/ppermute | solution.py:15
  120.0 43.9 %collective-permute-start.8 = (f32[2,128,12,128]{3,1,2,0:T(8,128)}, f32[2,128,12,128]{3,1,2,0:T(8,128)}, u32[]{:S(2)}, u32[]{:S(2)}) collective-permute-start(f32[2,128,12,128]{3,1,2,0:T(8,128)} %copy.71), channel_id=1, source_target_pairs={{0,252},{4,0},{8,4},{12,8},{16,12},{20,16},{24,20},{28,24},{32,28}... | collective-permute-start | bytes 4718600 | tf_op jit(solution)/shard_map/ppermute | solution.py:15
  125.2 27.0 %collective-permute-start = (f32[12]{0:T(128)S(1)}, f32[12]{0:T(128)S(1)}, u32[]{:S(2)}, u32[]{:S(2)}) collective-permute-start(f32[12]{0:T(128)S(1)} %convert_bitcast_fusion.4), channel_id=1, source_target_pairs={{0,248},{4,252},{8,0},{12,4},{16,8},{20,12},{24,16},{28,20},{32,24... | collective-permute-start | bytes 152 | tf_op jit(solution)/shard_map/ppermute | solution.py:15
  130.4 36.0 %collective-permute-start.9 = (f32[2,128,12,128]{3,1,2,0:T(8,128)}, f32[2,128,12,128]{3,1,2,0:T(8,128)}, u32[]{:S(2)}, u32[]{:S(2)}) collective-permute-start(f32[2,128,12,128]{3,1,2,0:T(8,128)} %copy.75), channel_id=1, source_target_pairs={{0,4},{4,8},{8,12},{12,16},{16,20},{20,24},{24,28},{28,32},{32,36}... | collective-permute-start | bytes 4718600 | tf_op jit(solution)/shard_map/ppermute | solution.py:15
  150.5 45.6 %collective-permute-start.10 = (f32[2,128,12,128]{3,1,2,0:T(8,128)}, f32[2,128,12,128]{3,1,2,0:T(8,128)}, u32[]{:S(2)}, u32[]{:S(2)}) collective-permute-start(f32[2,128,12,128]{3,1,2,0:T(8,128)} %copy.78), channel_id=1, source_target_pairs={{0,8},{4,12},{8,16},{12,20},{16,24},{20,28},{24,32},{28,36},{32,40... | collective-permute-start | bytes 4718600 | tf_op jit(solution)/shard_map/ppermute | solution.py:15
Sparse Core Ops, SparseCore 0:
  15.6 123.0 all-gather.2

commit v2 on v1

--- a/solution.py
+++ b/solution.py
@@ -59,22 +59,16 @@
     own_cols = b_cols[0]
     slot_ids = jnp.arange(c_cols.shape[1], dtype=jnp.int32)
     pattern = jnp.where(slot_ids[None, :] < c_count[:, None], c_cols, -1)
-    col_tags = own_cols.astype(jnp.float32)
-    arrived = []
-    sender_cols = []
+    wanted = []
     for hop_index in range(spread):
         shift_by = hop_index - REACH
-        if shift_by == 0:
-            arrived.append(partial_value[hop_index])
-            sender_cols.append(own_cols)
-        else:
-            moved, moved_tags = shifted((partial_value[hop_index], col_tags), "rows", shift_by)
-            arrived.append(moved)
-            sender_cols.append(moved_tags.astype(jnp.int32))
-    arrived = jnp.stack(arrived)
-    sender_cols = jnp.stack(sender_cols)
-    weights = (pattern[:, :, None, None] == sender_cols[None, None, :, :]).astype(jnp.float32)
-    result = jnp.einsum("ucdt,duatb->ucab", weights, arrived, precision=highest)
+        wanted.append(pattern if shift_by == 0 else shifted(pattern, "rows", -shift_by))
+    wanted = jnp.stack(wanted).reshape(spread, rows_dev, c_cols.shape[1])
+    weights = (wanted[:, :, :, None] == own_cols[None, None, None, :]).astype(jnp.float32)
+    mapped = jnp.einsum("huct,huatb->hucab", weights, partial_value, precision=highest)
+    result = mapped[REACH]
+    for shift_by in (2, -2, 1, -1):
+        result = result + shifted(mapped[shift_by + REACH], "rows", shift_by)
     before = jnp.cumsum(c_count, dtype=jnp.int32) - c_count
     row_start = earlier_counts(c_count) + before
     return (result, row_start)

time: 215 us -> 191 us (0.89)
  the two profiles are of different devices: /device:TPU:1 before, /device:TPU:16 now
where the time goes in v2:
time: 191 us; the launch traced here: 190 us
  waiting for transfers between devices  80 us (42%)
  local copies, waits for them, and re-layouts  33.9 us (18%)
  matrix products  33.8 us (18%)
  starting transfers between devices  19.2 us (10%)
  between operations  14.1 us (7%)
  other arithmetic  9.32 us (5%)
    ppermute x11, waiting for transfers between devices, shifted(): lax.ppermute(value, axis, [(i, (i + by) % size) for i in range(size)])  80 us
    dot_general x4, matrix products, chunk_product(): lax.dot_general(a_chunk, b_flat, (((1, 3), (0, 1)), ((), ())), precision=...  27.3 us
    ppermute x11, starting transfers between devices, shifted(): lax.ppermute(value, axis, [(i, (i + by) % size) for i in range(size)])  19.2 us
    reshape x1, local copies, waits for them, and re-layouts, local(): partial_value.reshape(spread, rows_dev, block_edge, b_slots, block_edge)  11.5 us
    unnamed x21, local copies, waits for them, and re-layouts  10.4 us
    add x1, local copies, waits for them, and re-layouts, local(): partial_value + chunk_product(arrived_b, (place - by) % n_rep)  9.09 us
    dot_general x1, matrix products, local(): jnp.einsum('huct,huatb->hucab', weights, partial_value, precision=highest)  6.55 us
    reduce_sum x1, other arithmetic, local(): jnp.sum(jnp.where(hit[:, :, :, None, None], blocks[None], 0.0), axis=2)  4.66 us
  transfers between devices with their start and end apart: 12, of which 4 were waited for; matrix products, arithmetic and copies ran while one was open for 36% of the time, Pallas kernels for 0%

profile of v2, /device:TPU:16, one launch (start us, length us, event | category | flops | bytes accessed | tf_op | source)
XLA Modules:
  0.0 190.3 jit_solution(1388953732811369987)
XLA Ops:
  7.2 0.0 all-gather.3.cloned.1.call-start
  7.2 0.8 compare_select_fusion
  8.0 7.5 %collective-permute-start.2 = (s32[2,8]{1,0:T(2,128)S(1)}, s32[2,8]{1,0:T(2,128)S(1)}, u32[]{:S(2)}, u32[]{:S(2)}) collective-permute-start(s32[2,8]{1,0:T(2,128)S(1)} %compare_select_fusion), channel_id=1, source_target_pairs={{0,252},{4,0},{8,4},{12,8},{16,12},{20,16},{24,20},{28,24},{32,28}... | collective-permute-start | bytes 200 | tf_op jit(solution)/shard_map/ppermute | solution.py:15
  15.5 1.0 collective-permute-start.3
  16.5 0.0 collective-permute-start.1
  16.5 1.0 collective-permute-start
  17.5 1.2 pad_bitcast_fusion
  18.7 0.0 all-gather.3.cloned.1.call-update
  18.8 1.9 copy.38
  20.6 0.4 collective-permute-start.5
  21.1 0.8 copy.37
  21.8 4.7 %select_reduce_fusion = f32[10,8,128,128]{3,2,1,0:T(8,128)S(1)} fusion(f32[8,4,128,128]{3,2,1,0:T(8,128)} %bitcast.85, pred[10,8,4]{2,1,0:T(8,128)(4,1)S(1)} %iota_compare_fusion), kind=kLoop, calls=%fused_computation | loop fusion | flops 9175040 | bytes 7340352 | tf_op jit(solution)/shard_map/reduce_sum | solution.py:40
  26.5 0.0 copy-start
  26.5 2.3 %copy-done = f32[10,8,128,128]{3,2,1,0:T(8,128)} copy-done((f32[10,8,128,128]{3,2,1,0:T(8,128)}, f32[10,8,128,128]{3,2,1,0:T(8,128)S(1)}, u32[]{:S(2)}) %copy-start) | copy-done | bytes 5242904
  28.9 0.0 copy-start.2
  28.9 0.0 copy-start.3
  28.9 5.5 %fusion.5 = f32[10,128,1536,1]{2,1,3,0:T(8,128)} fusion(f32[2,128,1536,1]{1,2,0,3:T(8,128)S(1)} %bitcast.84, f32[10,8,128,128]{3,2,1,0:T(8,128)S(1)} %select_reduce_fusion, s32[]{:T(128)S(6)} %select_n.42), kind=kOutput, calls=%fused_computation.9 | convolution fusion | flops 3019898880 | bytes 10747908 | tf_op jit(solution)/shard_map/dot_general | solution.py:45
  34.4 0.0 collective-permute-done
  34.4 2.2 %collective-permute-start.4 = (f32[2,128,12,128]{1,3,2,0:T(8,128)S(1)}, f32[2,128,12,128]{1,3,2,0:T(8,128)S(1)}, u32[]{:S(2)}, u32[]{:S(2)}) collective-permute-start(f32[2,128,12,128]{1,3,2,0:T(8,128)S(1)} %copy.38), channel_id=1, source_target_pairs={{0,1},{1,2},{2,3},{3,0},{4,5},{5,6},{6,7},{7,4},{8,9},{9,10},{10,1... | collective-permute-start | bytes 4718600 | tf_op jit(solution)/shard_map/ppermute | solution.py:15
  36.6 0.0 collective-permute-done.1
  36.6 0.5 collective-permute-start.6
  37.1 0.0 copy-done.2
  37.1 0.0 copy-done.3
  37.1 0.1 constant_dynamic-update-slice_fusion.2
  37.2 0.0 collective-permute-done.2
  37.2 0.0 collective-permute-done.3
  37.2 22.5 %collective-permute-done.5 = f32[2,128,12,128]{1,3,2,0:T(8,128)} collective-permute-done((f32[2,128,12,128]{1,3,2,0:T(8,128)S(1)}, f32[2,128,12,128]{1,3,2,0:T(8,128)}, u32[]{:S(2)}, u32[]{:S(2)}) %collective-permute-start.5) | collective-permute-done | bytes 1572896 | tf_op jit(solution)/shard_map/ppermute | solution.py:15
  59.7 5.4 %fusion.1 = f32[10,128,1536,1]{2,1,3,0:T(8,128)S(1)} fusion(f32[2,128,1536,1]{1,2,0,3:T(8,128)} %bitcast.19, f32[10,8,128,128]{3,2,1,0:T(8,128)} %copy-done, s32[]{:T(128)S(6)} %select_n.46), kind=kOutput, calls=%fused_computation.5 | convolution fusion | flops 3019898880 | bytes 10747908 | tf_op jit(solution)/shard_map/dot_general | solution.py:45
  65.1 27.5 %collective-permute-done.4 = f32[2,128,12,128]{1,3,2,0:T(8,128)S(1)} collective-permute-done((f32[2,128,12,128]{1,3,2,0:T(8,128)S(1)}, f32[2,128,12,128]{1,3,2,0:T(8,128)S(1)}, u32[]{:S(2)}, u32[]{:S(2)}) %collective-permute-start.4) | collective-permute-done | bytes 1572896 | tf_op jit(solution)/shard_map/ppermute | solution.py:15
  92.7 0.0 slice-start
  92.7 0.0 slice-start.1
  92.7 7.0 %fusion.3 = f32[10,128,1536,1]{2,1,3,0:T(8,128)} fusion(f32[2,128,1536,1]{1,2,0,3:T(8,128)S(1)} %bitcast.87, f32[10,8,128,128]{3,2,1,0:T(8,128)} %copy-done, s32[]{:T(128)S(6)} %select_n.44), kind=kOutput, calls=%fused_computation.7 | convolution fusion | flops 3019898880 | bytes 10747908 | tf_op jit(solution)/shard_map/dot_general | solution.py:45
  99.7 0.0 collective-permute-done.6
  99.7 0.0 slice-done
  99.7 0.0 slice-done.1
  99.7 9.3 %bitcast_add_fusion = f32[10,128,1536]{2,1,0:T(8,128)} fusion(f32[10,128,1536,1]{2,1,3,0:T(8,128)S(1)} %fusion.1, f32[10,128,1536,1]{2,1,3,0:T(8,128)} %fusion.3, f32[10,128,1536,1]{2,1,3,0:T(8,128)S(1)} %bitcast.82, f32[2,128,1536,1]{1,2,0,3:T(8,128)S(1)} %bitcast.86, f32[10,8,128,128]{3,2,1,0:T(8,128)} %copy-done, s32[]{:T(128)S(6)} %select_n.48), kind=kOutput, calls=%fused_computation.1 | convolution fusion | flops 3025797120 | bytes 34340868 | tf_op jit(solution)/shard_map/dot_general | solution.py:45
  109.0 9.1 %copy.46 = f32[10,128,1536]{1,2,0:T(8,128)} copy(f32[10,128,1536]{2,1,0:T(8,128)} %bitcast_add_fusion) | data formatting | bytes 15728640 | tf_op jit(solution)/shard_map/add | solution.py:56
  118.1 0.0 copy-start.4
  118.1 11.5 %copy.47 = f32[5,2,128,12,128]{4,3,2,1,0:T(8,128)} copy(f32[5,2,128,12,128]{2,4,3,1,0:T(8,128)} %bitcast.83) | data formatting | bytes 15728640 | tf_op jit(solution)/shard_map/reshape | solution.py:57
  129.5 0.0 copy-done.4
  129.5 6.6 %fusion.12 = f32[5,2,8,128,128]{4,2,3,1,0:T(8,128)S(1)} fusion(f32[5,2,128,12,128]{4,3,2,1,0:T(8,128)} %copy.47, s32[12]{0:T(128)S(1)} %bitcast.92, s32[5,2,8]{2,1,0:T(2,128)S(1)} %constant_dynamic-update-slice_fusion), kind=kOutput, calls=%fused_computation.25 | convolution fusion | flops 188744640 | bytes 13107568 | tf_op jit(solution)/shard_map/huct,huatb->hucab/dot_general | solution.py:68
  136.1 0.0 copy-start.1
  136.1 2.3 %copy-done.1 = f32[5,2,8,128,128]{4,2,3,1,0:T(8,128)} copy-done((f32[5,2,8,128,128]{4,2,3,1,0:T(8,128)}, f32[5,2,8,128,128]{4,2,3,1,0:T(8,128)S(1)}, u32[]{:S(2)}) %copy-start.1) | copy-done | bytes 5242904
  138.5 2.1 %slice_bitcast_fusion.3 = (f32[2,8,128,128]{3,1,2,0:T(8,128)}, f32[2,8,128,128]{3,1,2,0:T(8,128)}, f32[2,8,128,128]{3,1,2,0:T(8,128)}, f32[2,8,128,128]{3,1,2,0:T(8,128)}) fusion(f32[5,2,8,128,128]{4,2,3,1,0:T(8,128)S(1)} %fusion.12), kind=kLoop, calls=%fused_computation.14 | loop fusion | bytes 8388608 | tf_op jit(solution)/shard_map/squeeze | solution.py:71
  140.5 0.0 collective-permute-start.7
  140.6 4.8 %collective-permute-start.10 = (f32[2,8,128,128]{3,1,2,0:T(8,128)}, f32[2,8,128,128]{3,1,2,0:T(8,128)S(1)}, u32[]{:S(2)}, u32[]{:S(2)}) collective-permute-start(f32[2,8,128,128]{3,1,2,0:T(8,128)} %get-tuple-element.23), channel_id=1, source_target_pairs={{0,252},{4,0},{8,4},{12,8},{16,12},{20,16},{24,20},{28,24},{32,28}... | collective-permute-start | bytes 3145736 | tf_op jit(solution)/shard_map/ppermute | solution.py:15
  145.4 0.0 collective-permute-start.9
  145.4 1.7 collective-permute-start.8
  147.1 0.2 reduce-window.9
  147.3 0.0 all-gather.3.cloned.1.call-done
  147.3 1.4 copy.64
  148.7 0.7 fusion.11
  149.5 1.1 fusion.21
  150.6 19.5 %collective-permute-done.7 = f32[2,8,128,128]{3,1,2,0:T(8,128)S(1)} collective-permute-done((f32[2,8,128,128]{3,1,2,0:T(8,128)}, f32[2,8,128,128]{3,1,2,0:T(8,128)S(1)}, u32[]{:S(2)}, u32[]{:S(2)}) %collective-permute-start.7) | collective-permute-done | bytes 1048608 | tf_op jit(solution)/shard_map/ppermute | solution.py:15
  170.1 0.0 collective-permute-done.10
  170.1 10.4 %collective-permute-done.9 = f32[2,8,128,128]{3,1,2,0:T(8,128)S(1)} collective-permute-done((f32[2,8,128,128]{3,1,2,0:T(8,128)}, f32[2,8,128,128]{3,1,2,0:T(8,128)S(1)}, u32[]{:S(2)}, u32[]{:S(2)}) %collective-permute-start.9) | collective-permute-done | bytes 1048608 | tf_op jit(solution)/shard_map/ppermute | solution.py:15
  180.5 0.0 collective-permute-done.8
  180.5 1.8 fusion.10
  182.3 1.2 copy.48
  (6 shorter events, 0.0 us)
Async XLA Ops:
  7.2 140.1 %all-gather.3.cloned.1.call-start = ((), (), s32[]{:S(2)}) async-start(), calls=%async_computation | async-start | bytes 1052672 | tf_op jit(solution)/shard_map/all_gather | solution.py:20
  8.0 29.2 %collective-permute-start.2 = (s32[2,8]{1,0:T(2,128)S(1)}, s32[2,8]{1,0:T(2,128)S(1)}, u32[]{:S(2)}, u32[]{:S(2)}) collective-permute-start(s32[2,8]{1,0:T(2,128)S(1)} %compare_select_fusion), channel_id=1, source_target_pairs={{0,252},{4,0},{8,4},{12,8},{16,12},{20,16},{24,20},{28,24},{32,28}... | collective-permute-start | bytes 200 | tf_op jit(solution)/shard_map/ppermute | solution.py:15
  15.5 21.7 %collective-permute-start.3 = (s32[2,8]{1,0:T(2,128)S(1)}, s32[2,8]{1,0:T(2,128)S(1)}, u32[]{:S(2)}, u32[]{:S(2)}) collective-permute-start(s32[2,8]{1,0:T(2,128)S(1)} %compare_select_fusion), channel_id=1, source_target_pairs={{0,248},{4,252},{8,0},{12,4},{16,8},{20,12},{24,16},{28,20},{32,24... | collective-permute-start | bytes 200 | tf_op jit(solution)/shard_map/ppermute | solution.py:15
  16.5 20.1 %collective-permute-start.1 = (s32[2,8]{1,0:T(2,128)S(1)}, s32[2,8]{1,0:T(2,128)S(1)}, u32[]{:S(2)}, u32[]{:S(2)}) collective-permute-start(s32[2,8]{1,0:T(2,128)S(1)} %compare_select_fusion), channel_id=1, source_target_pairs={{0,4},{4,8},{8,12},{12,16},{16,20},{20,24},{24,28},{28,32},{32,36}... | collective-permute-start | bytes 200 | tf_op jit(solution)/shard_map/ppermute | solution.py:15
  16.5 17.9 %collective-permute-start = (s32[2,8]{1,0:T(2,128)S(1)}, s32[2,8]{1,0:T(2,128)S(1)}, u32[]{:S(2)}, u32[]{:S(2)}) collective-permute-start(s32[2,8]{1,0:T(2,128)S(1)} %compare_select_fusion), channel_id=1, source_target_pairs={{0,8},{4,12},{8,16},{12,20},{16,24},{20,28},{24,32},{28,36},{32,40... | collective-permute-start | bytes 200 | tf_op jit(solution)/shard_map/ppermute | solution.py:15
  20.6 39.0 %collective-permute-start.5 = (f32[2,128,12,128]{1,3,2,0:T(8,128)S(1)}, f32[2,128,12,128]{1,3,2,0:T(8,128)}, u32[]{:S(2)}, u32[]{:S(2)}) collective-permute-start(f32[2,128,12,128]{1,3,2,0:T(8,128)S(1)} %copy.38), channel_id=1, source_target_pairs={{0,2},{1,3},{2,0},{3,1},{4,6},{5,7},{6,4},{7,5},{8,10},{9,11},{10,... | collective-permute-start | bytes 4718600 | tf_op jit(solution)/shard_map/ppermute | solution.py:15
  26.5 2.4 %copy-start = (f32[10,8,128,128]{3,2,1,0:T(8,128)}, f32[10,8,128,128]{3,2,1,0:T(8,128)S(1)}, u32[]{:S(2)}) copy-start(f32[10,8,128,128]{3,2,1,0:T(8,128)S(1)} %select_reduce_fusion) | copy-start | bytes 15728644
  28.9 8.2 %copy-start.2 = (s32[2]{0:T(128)S(1)}, s32[2]{0:T(128)}, u32[]{:S(2)}) copy-start(s32[2]{0:T(128)} %param.13) | copy-start | bytes 28
  28.9 8.2 %copy-start.3 = (s32[2,8]{1,0:T(2,128)S(1)}, s32[2,8]{1,0:T(2,128)}, u32[]{:S(2)}) copy-start(s32[2,8]{1,0:T(2,128)} %param.12) | copy-start | bytes 196
  34.4 58.3 %collective-permute-start.4 = (f32[2,128,12,128]{1,3,2,0:T(8,128)S(1)}, f32[2,128,12,128]{1,3,2,0:T(8,128)S(1)}, u32[]{:S(2)}, u32[]{:S(2)}) collective-permute-start(f32[2,128,12,128]{1,3,2,0:T(8,128)S(1)} %copy.38), channel_id=1, source_target_pairs={{0,1},{1,2},{2,3},{3,0},{4,5},{5,6},{6,7},{7,4},{8,9},{9,10},{10,1... | collective-permute-start | bytes 4718600 | tf_op jit(solution)/shard_map/ppermute | solution.py:15
  36.6 63.1 %collective-permute-start.6 = (f32[2,128,12,128]{1,3,2,0:T(8,128)S(1)}, f32[2,128,12,128]{1,3,2,0:T(8,128)S(1)}, u32[]{:S(2)}, u32[]{:S(2)}) collective-permute-start(f32[2,128,12,128]{1,3,2,0:T(8,128)S(1)} %copy.38), channel_id=1, source_target_pairs={{0,3},{1,0},{2,1},{3,2},{4,7},{5,4},{6,5},{7,6},{8,11},{9,8},{10,9... | collective-permute-start | bytes 4718600 | tf_op jit(solution)/shard_map/ppermute | solution.py:15
  92.7 7.0 %slice-start = ((s8[7864320]{0:T(1024)(128)(4,1)}), s8[4194304]{0:T(1024)(128)(4,1)S(1)}, s32[]{:S(2)}) async-start(s8[7864320]{0:T(1024)(128)(4,1)} %bitcast.81), calls=%async_computation.1 | async-start | bytes 8388608
  92.7 7.0 %slice-start.1 = ((s8[7864320]{0:T(1024)(128)(4,1)}), s8[3670016]{0:T(1024)(128)(4,1)S(1)}, s32[]{:S(2)}) async-start(s8[7864320]{0:T(1024)(128)(4,1)} %bitcast.81), calls=%async_computation.2 | async-start | bytes 7340032
  118.1 11.5 %copy-start.4 = (s32[1,12]{1,0:T(1,128)S(1)}, s32[1,12]{1,0:T(1,128)}, u32[]{:S(2)}) copy-start(s32[1,12]{1,0:T(1,128)} %param.11) | copy-start | bytes 148
  136.1 2.4 %copy-start.1 = (f32[5,2,8,128,128]{4,2,3,1,0:T(8,128)}, f32[5,2,8,128,128]{4,2,3,1,0:T(8,128)S(1)}, u32[]{:S(2)}) copy-start(f32[5,2,8,128,128]{4,2,3,1,0:T(8,128)S(1)} %fusion.12) | copy-start | bytes 15728644
  140.5 29.6 %collective-permute-start.7 = (f32[2,8,128,128]{3,1,2,0:T(8,128)}, f32[2,8,128,128]{3,1,2,0:T(8,128)S(1)}, u32[]{:S(2)}, u32[]{:S(2)}) collective-permute-start(f32[2,8,128,128]{3,1,2,0:T(8,128)} %get-tuple-element.22), channel_id=1, source_target_pairs={{0,8},{4,12},{8,16},{12,20},{16,24},{20,28},{24,32},{28,36},{32,40... | collective-permute-start | bytes 3145736 | tf_op jit(solution)/shard_map/ppermute | solution.py:15
  140.6 29.6 %collective-permute-start.10 = (f32[2,8,128,128]{3,1,2,0:T(8,128)}, f32[2,8,128,128]{3,1,2,0:T(8,128)S(1)}, u32[]{:S(2)}, u32[]{:S(2)}) collective-permute-start(f32[2,8,128,128]{3,1,2,0:T(8,128)} %get-tuple-element.23), channel_id=1, source_target_pairs={{0,252},{4,0},{8,4},{12,8},{16,12},{20,16},{24,20},{28,24},{32,28}... | collective-permute-start | bytes 3145736 | tf_op jit(solution)/shard_map/ppermute | solution.py:15
  145.4 35.2 %collective-permute-start.9 = (f32[2,8,128,128]{3,1,2,0:T(8,128)}, f32[2,8,128,128]{3,1,2,0:T(8,128)S(1)}, u32[]{:S(2)}, u32[]{:S(2)}) collective-permute-start(f32[2,8,128,128]{3,1,2,0:T(8,128)} %get-tuple-element.24), channel_id=1, source_target_pairs={{0,4},{4,8},{8,12},{12,16},{16,20},{20,24},{24,28},{28,32},{32,36}... | collective-permute-start | bytes 3145736 | tf_op jit(solution)/shard_map/ppermute | solution.py:15
  145.4 35.2 %collective-permute-start.8 = (f32[2,8,128,128]{3,1,2,0:T(8,128)}, f32[2,8,128,128]{3,1,2,0:T(8,128)}, u32[]{:S(2)}, u32[]{:S(2)}) collective-permute-start(f32[2,8,128,128]{3,1,2,0:T(8,128)} %get-tuple-element.25), channel_id=1, source_target_pairs={{0,248},{4,252},{8,0},{12,4},{16,8},{20,12},{24,16},{28,20},{32,24... | collective-permute-start | bytes 3145736 | tf_op jit(solution)/shard_map/ppermute | solution.py:15
Sparse Core Ops, SparseCore 0:
  18.9 116.1 all-gather.2
